TPU v7x, 128 devices: a whole 4x4x4 slice. The times are simulated.
128 devices in a mesh: seq: 16 (over z, y), tp: 8 (over x, core).
Axes of the slice: x: 4, y: 4, z: 4, core: 2. Of those that a mesh axis runs over, the one named last changes fastest.
Arguments:
- hidden: bfloat16 [128, 64, 2560], P(None, 'seq'), may hold values from -6 to 6
- gain_attn: bfloat16 [2560], replicated, may hold values from 0.099609375 to 1.8984375
- w_query: bfloat16 [2560, 2560], P(None, 'tp'), may hold values from -0.125 to 0.125
- w_key: bfloat16 [2560, 640], P(None, 'tp'), may hold values from -0.375 to 0.375
- w_value: bfloat16 [2560, 640], P(None, 'tp'), may hold values from -0.25 to 0.25
- w_out: bfloat16 [2560, 2560], P('tp'), may hold values from -0.125 to 0.125
- gain_ffn: bfloat16 [2560], replicated, may hold values from 0.099609375 to 1.8984375
- w_gate: bfloat16 [2560, 6912], P(None, 'tp'), may hold values from -0.125 to 0.125
- w_up: bfloat16 [2560, 6912], P(None, 'tp'), may hold values from -0.125 to 0.125
- w_down: bfloat16 [6912, 2560], P('tp'), may hold values from -0.078125 to 0.078125
- shared_pages: bfloat16 [320, 8, 2, 80, 128], P('seq', 'tp'), may hold values from -270 to 270
- leaf_pages: bfloat16 [512, 8, 2, 80, 128], P('seq', 'tp'), may hold values from -270 to 270
- root_table: int32 [4, 16], replicated, may hold values from 0 to 319, as said below
- mid_table: int32 [16, 16], replicated, may hold values from 0 to 319, as said below
- leaf_table: int32 [64, 8], replicated, may hold values from 0 to 511, as said below
- root_len: int32 [4], replicated, may hold values from 1024 to 2048, as said below
- mid_len: int32 [16], replicated, may hold values from 1 to 2048, as said below
- leaf_len: int32 [64], replicated, may hold values from 1 to 1024, as said below
- mid_parent: int32 [16], replicated, may hold values from 0 to 3
- leaf_parent: int32 [64], replicated, may hold values from 0 to 15
- slot_request: int32 [64], replicated, may hold values from 0 to 63, as said below
Outputs:
- layer_out: float32 [128, 64, 2560], P('tp', 'seq')
Inputs may be any that keep to these rules, and one draw needn't show every extreme that they name: `slot_request`: A permutation of the requests. The 4 requests of slots 4 * s to 4 * s + 3 have their leaves with 4 distinct owners (see leaf_table). `leaf_table`: all pages of one request's leaf lie with one owner, the index of seq equal to page // 32; each owner holds the leaves of exactly 4 requests, and every leaf page is named once. `root_table`: with mid_table, names every shared page exactly once. Shared page g is held by the index of seq g // 20; each index holds exactly 1 page of every root. `mid_table`: with root_table, names every shared page exactly once. Each index of seq holds exactly 1 page of every middle node. `root_len`: some root reaches the largest value. `mid_len`: some middle node reaches the largest value. `leaf_len`: some leaf reaches the largest value.
All inputs are finite; a program needn't handle non-finite values.
Results may differ from a plain program's by a relative error of at most 0.009.
The roundings to bfloat16 on the way count: a program that leaves them out, or rounds other values in their place, can miss the bound.
Values may be sent and summed in bfloat16 or wider, within the bound.
No kernel may reach another device: no remote copies, remote signals or barrier semaphores. Data moves between devices by JAX's collectives and lax.ppermute only.
A program may use at most 192 MiB of HBM per device.

v0:
```python
import jax
import jax.numpy as jnp
from jax import lax
from jax.sharding import PartitionSpec as P

QH = 32
KVH = 8
HD = 80
WINDOW = 4096
masked_score = -1e30
rope_base = 10000.0


def rms_norm(row_data, gain_vector):
    values = row_data.astype(jnp.float32)
    inverse_rms = lax.rsqrt(jnp.mean(values * values, -1, keepdims=True) + 1e-05)
    return (values * inverse_rms * gain_vector.astype(jnp.float32)).astype(jnp.bfloat16)


def rotate(vector, position):
    half_size = vector.shape[-1] // 2
    frequency = rope_base ** (-2.0 * jnp.arange(half_size, dtype=jnp.float32) / vector.shape[-1])
    angles = position.astype(jnp.float32)[..., None] * frequency
    cos_part = jnp.cos(angles)
    sin_part = jnp.sin(angles)
    first_half = vector[..., :half_size]
    second_half = vector[..., half_size:]
    return jnp.concatenate(
        [
            first_half * cos_part - second_half * sin_part,
            second_half * cos_part + first_half * sin_part,
        ],
        -1,
    )


def page_columns(pages):
    moved = jnp.moveaxis(pages, -5, -2)
    return moved.reshape(moved.shape[:-2] + (moved.shape[-2] * moved.shape[-1],))


def attend(queries, key_pack, key_pos, present, query_pos):
    scores = jnp.einsum(
        "nbkge,bket->nbkgt", queries, key_pack[:, :, 0], preferred_element_type=jnp.float32
    ) * queries.shape[-1] ** (-0.5)
    distance = query_pos[:, :, None] - key_pos[None, :, :]
    allowed = (present[None, :, :] & (distance >= 0) & (distance < WINDOW))[:, :, None, None, :]
    scores = jnp.where(allowed, scores, masked_score)
    maximum = jnp.max(scores, -1)
    weights = jnp.where(allowed, jnp.exp(scores - maximum[..., None]), 0.0)
    totals = jnp.sum(weights, -1)
    weighted = jnp.einsum(
        "nbkgt,bket->nbkge",
        weights.astype(jnp.bfloat16),
        key_pack[:, :, 1],
        preferred_element_type=jnp.float32,
    )
    return (weighted, maximum, totals)


def merge_parts(first, second):
    maximum = jnp.maximum(first[1], second[1])
    first_scale = jnp.exp(first[1] - maximum)
    second_scale = jnp.exp(second[1] - maximum)
    return (
        first[0] * first_scale[..., None] + second[0] * second_scale[..., None],
        maximum,
        first[2] * first_scale + second[2] * second_scale,
    )


def spans(request_ids, root_len, mid_len, leaf_len, mid_parent, leaf_parent):
    mid_nodes = leaf_parent[request_ids]
    root_nodes = mid_parent[mid_nodes]
    return (root_nodes, mid_nodes, root_len[root_nodes], mid_len[mid_nodes], leaf_len[request_ids])


def shards(
    hidden,
    gain_attn,
    w_query,
    w_key,
    w_value,
    w_out,
    gain_ffn,
    w_gate,
    w_up,
    w_down,
    shared_pages,
    leaf_pages,
    root_table,
    mid_table,
    leaf_table,
    root_len,
    mid_len,
    leaf_len,
    mid_parent,
    leaf_parent,
    slot_request,
):
    new_rows, local_reqs, model_width = hidden.shape
    seq_count = lax.axis_size("seq")
    seq_index = lax.axis_index("seq")
    kv_local = leaf_pages.shape[1]
    group_size = QH // KVH
    pages_here = leaf_pages.shape[0]
    slot_ids = seq_index * local_reqs + jnp.arange(local_reqs, dtype=jnp.int32)
    requests = slot_request[slot_ids]
    root_nodes, mid_nodes, root_span, mid_span, leaf_span = spans(
        requests, root_len, mid_len, leaf_len, mid_parent, leaf_parent
    )
    context = root_span + mid_span + leaf_span
    new_index = jnp.arange(new_rows, dtype=jnp.int32)
    query_pos = context[None, :] + new_index[:, None]
    all_slots = slot_request.reshape(seq_count, local_reqs)
    page_store = lax.all_gather(shared_pages, "seq", axis=0, tiled=True)
    root_index = root_table[root_nodes]
    mid_index = mid_table[mid_nodes]
    normed = rms_norm(hidden, gain_attn).reshape(-1, model_width)
    query_proj = jnp.dot(normed, w_query, preferred_element_type=jnp.float32).reshape(
        new_rows, local_reqs, -1, HD
    )
    queries = (
        rotate(query_proj, query_pos[:, :, None])
        .astype(jnp.bfloat16)
        .reshape(new_rows, local_reqs, kv_local, group_size, HD)
    )
    key_proj = jnp.dot(normed, w_key, preferred_element_type=jnp.float32).reshape(
        new_rows, local_reqs, kv_local, HD
    )
    new_keys = rotate(key_proj, query_pos[:, :, None]).astype(jnp.bfloat16)
    new_values = (
        jnp.dot(normed, w_value, preferred_element_type=jnp.float32)
        .astype(jnp.bfloat16)
        .reshape(new_rows, local_reqs, kv_local, HD)
    )
    home_of = leaf_table[:, 0] // pages_here
    own_homes = home_of[requests]
    sender_match = home_of[all_slots] == seq_index
    sender_pick = jnp.argmax(sender_match, 1)
    sender_have = jnp.any(sender_match, 1)
    picked_request = jnp.take_along_axis(all_slots, sender_pick[:, None], 1)[:, 0]
    page_ids = jnp.where(
        sender_have[:, None], leaf_table[picked_request] - seq_index * pages_here, 0
    )
    leaf_steps = jnp.arange(leaf_table.shape[1] * leaf_pages.shape[-1], dtype=jnp.int32)
    fresh_pack = jnp.stack(
        [jnp.transpose(new_keys, (1, 2, 3, 0)), jnp.transpose(new_values, (1, 2, 3, 0))], 2
    )
    fresh_part = attend(
        queries,
        fresh_pack,
        context[:, None] + new_index[None, :],
        jnp.ones((local_reqs, new_rows), bool),
        query_pos,
    )
    outgoing = jnp.where(
        sender_have[:, None, None, None, None, None], jnp.take(leaf_pages, page_ids, axis=0), 0
    )
    arrived = lax.all_to_all(outgoing, "seq", split_axis=0, concat_axis=0, tiled=True)
    leaf_pack = page_columns(jnp.take(arrived, own_homes, axis=0))
    leaf_pos = (root_span + mid_span)[:, None] + leaf_steps[None, :]
    leaf_part = attend(
        queries, leaf_pack, leaf_pos, leaf_steps[None, :] < leaf_span[:, None], query_pos
    )
    root_pack = page_columns(jnp.take(page_store, root_index, axis=0))
    root_steps = jnp.arange(root_pack.shape[-1], dtype=jnp.int32)
    root_part = attend(
        queries,
        root_pack,
        root_steps[None, :] + 0 * root_span[:, None],
        root_steps[None, :] < root_span[:, None],
        query_pos,
    )
    mid_pack = page_columns(jnp.take(page_store, mid_index, axis=0))
    mid_steps = jnp.arange(mid_pack.shape[-1], dtype=jnp.int32)
    mid_part = attend(
        queries,
        mid_pack,
        root_span[:, None] + mid_steps[None, :],
        mid_steps[None, :] < mid_span[:, None],
        query_pos,
    )
    combined = merge_parts(merge_parts(root_part, mid_part), merge_parts(leaf_part, fresh_part))
    attended = (
        (combined[0] / combined[2][..., None])
        .astype(jnp.bfloat16)
        .reshape(new_rows * local_reqs, -1)
    )
    tp_count = lax.axis_size("tp")
    own_count = new_rows // tp_count
    attn_proj = lax.psum_scatter(
        jnp.dot(attended, w_out, preferred_element_type=jnp.float32),
        "tp",
        scatter_dimension=0,
        tiled=True,
    ).reshape(own_count, local_reqs, model_width)
    own_hidden = lax.dynamic_slice_in_dim(hidden, lax.axis_index("tp") * own_count, own_count, 0)
    resid = own_hidden.astype(jnp.float32) + attn_proj
    normed_own = rms_norm(resid, gain_ffn).reshape(-1, model_width)
    normed_ffn = lax.all_gather(normed_own, "tp", axis=0, tiled=True)
    gate_rows = jnp.dot(normed_ffn, w_gate, preferred_element_type=jnp.float32)
    up_rows = jnp.dot(normed_ffn, w_up, preferred_element_type=jnp.float32)
    activated = (jax.nn.silu(gate_rows) * up_rows).astype(jnp.bfloat16)
    ffn_proj = lax.psum_scatter(
        jnp.dot(activated, w_down, preferred_element_type=jnp.float32),
        "tp",
        scatter_dimension=0,
        tiled=True,
    ).reshape(own_count, local_reqs, model_width)
    return resid + ffn_proj


def solution(mesh):
    return jax.shard_map(
        shards,
        mesh=mesh,
        in_specs=(
            P(None, "seq", None),
            P(),
            P(None, "tp"),
            P(None, "tp"),
            P(None, "tp"),
            P("tp", None),
            P(),
            P(None, "tp"),
            P(None, "tp"),
            P("tp", None),
            P("seq", "tp", None, None, None),
            P("seq", "tp", None, None, None),
            P(),
            P(),
            P(),
            P(),
            P(),
            P(),
            P(),
            P(),
            P(),
        ),
        out_specs=P("tp", "seq", None),
        check_vma=False,
    )
```

profile of v0, /device:TPU:0, one launch (start us, length us, event | category | flops | bytes accessed | tf_op | source)
XLA Modules:
  0.0 381.0 jit_solution(9774462938295240041)
XLA Ops:
  13.6 3.6 gather_fusion.11
  17.2 5.5 %select_select_fusion = bf16[16,8,1,2,80,128]{5,4,3,1,2,0:T(8,128)(2,1)} fusion(bf16[16,8,1,2,80,128]{5,4,3,1,2,0:T(8,128)(2,1)} %bitcast.319, pred[16]{0:T(512)(128)(4,1)S(1)} %reduce_or.9, pred[16,8]{1,0:T(8,128)(4,1)S(1)} %get-tuple-element.15), kind=kLoop, calls=%fused_computation.44 | loop fusion | flops 5242880 | bytes 10485904 | tf_op jit(solution)/shard_map/jit(_where)/select_n | solution.py:157
  22.7 8.3 %all-to-all-start = ((bf16[16,8,1,2,80,128]{5,4,3,1,2,0:T(8,128)(2,1)}), bf16[16,8,1,2,80,128]{5,4,3,1,2,0:T(8,128)(2,1)}, u32[]{:S(2)}, u32[]{:S(2)}) async-start(bf16[16,8,1,2,80,128]{5,4,3,1,2,0:T(8,128)(2,1)} %select_select_fusion), calls=%async_computation | async-start | bytes 10485760 | tf_op jit(solution)/shard_map/all_to_all | solution.py:160
  37.0 3.3 fusion.17
  40.4 3.0 fusion.19
  43.4 5.6 %reshape.793 = bf16[512,2560]{1,0:T(8,128)(2,1)} reshape(bf16[128,4,2560]{2,1,0:T(4,128)(2,1)} %fusion.19) | data formatting | bytes 5242880 | tf_op jit(solution)/shard_map/reshape | solution.py:119
  49.0 2.6 convolution_convert_fusion
  54.8 2.8 fusion.73
  65.7 5.5 %fusion.26 = (pred[128,4,2048]{0,2,1:T(8,128)(4,1)}, pred[128,4,2048]{0,2,1:T(8,128)(4,1)}) fusion(s32[128,4]{0,1:T(4,128)S(1)} %get-tuple-element.27, pred[4,2048]{1,0:T(4,128)(4,1)S(1)} %iota_compare_fusion.1, s32[4,2048]{1,0:T(4,128)S(1)} %iota_add_fusion, pred[4,2048]{1,0:T(4,128)(4,1)S(1)} %iota_compare_fusion), kind=kLoop, calls=%fused_computation.51 | loop fusion | flops 10485760 | bytes 2148352 | tf_op jit(solution)/shard_map/and | solution.py:47
  71.2 56.7 %all-to-all-done = bf16[16,8,1,2,80,128]{5,4,3,1,2,0:T(8,128)(2,1)} async-done(((bf16[16,8,1,2,80,128]{5,4,3,1,2,0:T(8,128)(2,1)}), bf16[16,8,1,2,80,128]{5,4,3,1,2,0:T(8,128)(2,1)}, u32[]{:S(2)}, u32[]{:S(2)}) %all-to-all-start) | async-done | bytes 5242912 | tf_op jit(solution)/shard_map/all_to_all | solution.py:160
  127.9 3.4 gather_fusion.12
  136.7 3.2 copy-done.10
  140.0 2.7 fusion.15
  142.7 15.5 %all-gather.3.cloned.1.call-done = bf16[320,1,2,80,128]{4,3,2,1,0:T(8,128)(2,1)} async-done(((bf16[20,1,2,80,128]{4,3,2,1,0:T(8,128)(2,1)}), bf16[320,1,2,80,128]{4,3,2,1,0:T(8,128)(2,1)}) %all-gather.3.cloned.1.call-update) | async-done | bytes 13107216 | tf_op jit(solution)/shard_map/all_gather | solution.py:116
  158.2 7.1 %gather_fusion.15 = bf16[64,2,80,128]{3,2,1,0:T(8,128)(2,1)} fusion(bf16[320,2,80,128]{3,2,1,0:T(8,128)(2,1)} %bitcast.325, s32[1024]{0:T(1024)S(1)} %copy-done.30), kind=kCustom, calls=%fused_computation.1.clone | custom fusion | bytes 5243136 | tf_op jit(solution)/shard_map/jit(_take)/gather | solution.py:175
  165.3 7.2 %gather_fusion.14 = bf16[64,2,80,128]{3,2,1,0:T(8,128)(2,1)} fusion(bf16[320,2,80,128]{3,2,1,0:T(8,128)(2,1)} %bitcast.326, s32[1024]{0:T(1024)S(1)} %copy-done.29), kind=kCustom, calls=%fused_computation.clone | custom fusion | bytes 5243136 | tf_op jit(solution)/shard_map/jit(_take)/gather | solution.py:166
  172.5 4.2 %fusion.35 = bf16[4,1,2,80,16,128]{5,4,3,0,2,1:T(8,128)(2,1)} fusion(bf16[4,16,1,2,80,128]{5,4,3,1,0,2:T(8,128)(2,1)} %bitcast.322, pred[4,16]{1,0:T(4,128)(4,1)S(1)} %copy-done.34), kind=kLoop, calls=%fused_computation.64 | loop fusion | flops 1310720 | bytes 5242944 | tf_op jit(solution)/shard_map/transpose | solution.py:38
  176.6 5.2 %reshape.777 = bf16[4,1,2,80,2048]{4,3,0,2,1:T(8,128)(2,1)} reshape(bf16[4,1,2,80,16,128]{5,4,3,0,2,1:T(8,128)(2,1)} %fusion.35) | data formatting | bytes 5242880 | tf_op jit(solution)/shard_map/reshape | solution.py:39
  181.8 4.3 %fusion.34 = bf16[4,1,2,80,16,128]{5,4,3,0,2,1:T(8,128)(2,1)} fusion(bf16[4,16,1,2,80,128]{5,4,3,1,0,2:T(8,128)(2,1)} %bitcast.321, pred[4,16]{1,0:T(4,128)(4,1)S(1)} %copy-done.33), kind=kLoop, calls=%fused_computation.62 | loop fusion | flops 1310720 | bytes 5242944 | tf_op jit(solution)/shard_map/transpose | solution.py:38
  186.1 5.2 %reshape.781 = bf16[4,1,2,80,2048]{4,3,0,2,1:T(8,128)(2,1)} reshape(bf16[4,1,2,80,16,128]{5,4,3,0,2,1:T(8,128)(2,1)} %fusion.34) | data formatting | bytes 5242880 | tf_op jit(solution)/shard_map/reshape | solution.py:39
  191.3 8.8 %fusion.1 = (f32[128,4,4]{0,2,1:T(4,128)S(1)}, f32[4,2048,128,4]{2,1,3,0:T(8,128)}) fusion(pred[128,4,2048]{0,2,1:T(8,128)(4,1)S(1)} %copy-done.12, bf16[128,4,4,40]{0,3,2,1:T(8,128)(2,1)S(1)} %copy-done.23, bf16[128,4,4,40]{0,3,2,1:T(8,128)(2,1)S(1)} %copy-done.21, bf16[4,1,2,80,2048]{4,3,0,2,1:T(8,128)(2,1)} %reshape.781), kind=kOutput, calls=%fused_computation.21 | convolution fusion | flops 684324864 | bytes 19472384 | tf_op jit(solution)/shard_map/nbkge,bket->nbkgt/dot_general | solution.py:43
  200.2 2.7 fusion
  203.0 10.7 %fusion.2 = (f32[128,4,4]{0,2,1:T(4,128)S(1)}, f32[128,4,4]{0,2,1:T(4,128)S(1)}) fusion(f32[4,2048,128,4]{2,1,3,0:T(8,128)S(1)} %get-tuple-element.36, f32[128,4,4]{0,2,1:T(4,128)S(1)} %get-tuple-element.35, pred[128,4,2048]{0,2,1:T(8,128)(4,1)S(1)} %copy-done.11, f32[128,4,4]{0,2,1:T(4,128)S(1)} %get-tuple-element.29, ...), kind=kLoop, calls=%fused_computation.22 | loop fusion | flops 41938944 | bytes 35684352 | tf_op jit(solution)/shard_map/reduce_sum | solution.py:51
  213.8 2.9 fusion.56
  216.7 10.7 %fusion.68 = f32[128,4,1,4,80]{0,4,3,1,2:T(8,128)} fusion(f32[4,2048,128,4]{2,1,3,0:T(8,128)} %get-tuple-element.30, f32[128,4,4]{0,2,1:T(4,128)S(1)} %get-tuple-element.29, pred[128,4,2048]{0,2,1:T(8,128)(4,1)S(1)} %copy-done.12, bf16[4,1,2,80,2048]{4,3,0,2,1:T(8,128)(2,1)} %reshape.781, f32[128,4,4]{0,2,1:T(4,128)S(1)} %bitcast.341), kind=kOutput, calls=%fused_computation.91 | convolution fusion | flops 692224000 | bytes 19808256 | tf_op jit(solution)/shard_map/nbkgt,bket->nbkge/dot_general | solution.py:52
  227.4 5.8 %fusion.65 = f32[128,4,1,4,80]{0,4,3,1,2:T(8,128)} fusion(f32[128,4,1,4,80]{0,4,3,1,2:T(8,128)} %fusion.68, f32[4,2048,128,4]{2,1,3,0:T(8,128)S(1)} %get-tuple-element.36, f32[128,4,4]{0,2,1:T(4,128)S(1)} %get-tuple-element.35, pred[128,4,2048]{0,2,1:T(8,128)(4,1)S(1)} %copy-done.11, bf16[4,1,2,80,2048]{4,3,0,2,1:T(8,128)(2,1)} %reshape.777, ...), kind=kOutput, calls=%fused_computation.90 | convolution fusion | flops 692551680 | bytes 20471808 | tf_op jit(solution)/shard_map/nbkgt,bket->nbkge/dot_general | solution.py:52
  235.7 3.8 %fusion.124 = f32[512,2560]{1,0:T(8,128)} fusion(bf16[512,320]{1,0:T(8,128)(2,1)S(1)} %reshape.797, bf16[320,2560]{1,0:T(8,128)(2,1)S(1)} %copy-done), kind=kOutput, calls=%fused_computation.213 | convolution fusion | flops 838860800 | bytes 7208960 | tf_op jit(solution)/shard_map/dot_general | solution.py:193
  240.2 40.4 %reduce-scatter.3.cloned.1.call-done = f32[64,2560]{1,0:T(8,128)} async-done(((f32[512,2560]{1,0:T(8,128)}), f32[64,2560]{1,0:T(8,128)}) %reduce-scatter.3.cloned.1.call-update) | async-done | bytes 655376 | tf_op jit(solution)/shard_map/reduce_scatter | solution.py:192
  285.5 25.5 %all-gather.5.cloned.1.call-done = bf16[512,2560]{1,0:T(8,128)(2,1)} async-done(((bf16[64,2560]{1,0:T(8,128)(2,1)}), bf16[512,2560]{1,0:T(8,128)(2,1)}) %all-gather.5.cloned.1.call-update) | async-done | bytes 2621456 | tf_op jit(solution)/shard_map/all_gather | solution.py:201
  311.0 6.8 %fusion.125 = f32[512,864]{0,1:T(8,128)} fusion(bf16[512,2560]{1,0:T(8,128)(2,1)} %all-gather.5.cloned.1.call-done, bf16[2560,864]{0,1:T(8,128)(2,1)} %param.30), kind=kOutput, calls=%fused_computation.214 | convolution fusion | flops 2264924160 | bytes 8814592 | tf_op jit(solution)/shard_map/dot_general | solution.py:202
  317.8 12.5 %fusion.78 = f32[512,2560]{1,0:T(8,128)} fusion(bf16[864,2560]{1,0:T(8,128)(2,1)} %param.32, f32[512,864]{0,1:T(8,128)} %fusion.125, bf16[512,2560]{1,0:T(8,128)(2,1)} %all-gather.5.cloned.1.call-done, bf16[2560,864]{0,1:T(8,128)(2,1)} %param.31), kind=kOutput, calls=%fused_computation.99 | convolution fusion | flops 4532502528 | bytes 18481152 | tf_op jit(solution)/shard_map/dot_general | solution.py:206
  330.3 40.6 %reduce-scatter.5.cloned.1.call-done = f32[64,2560]{1,0:T(8,128)} async-done(((f32[512,2560]{1,0:T(8,128)}), f32[64,2560]{1,0:T(8,128)}) %reduce-scatter.5.cloned.1.call-update) | async-done | bytes 655376 | tf_op jit(solution)/shard_map/reduce_scatter | solution.py:205
  (177 shorter events, 40.8 us)
Async XLA Ops:
  6.5 229.2 %copy-start = (bf16[320,2560]{1,0:T(8,128)(2,1)S(1)}, bf16[320,2560]{1,0:T(8,128)(2,1)}, u32[]{:S(2)}) copy-start(bf16[320,2560]{1,0:T(8,128)(2,1)} %param.28) | copy-start | bytes 4915204
  6.5 151.7 %all-gather.3.cloned.1.call-start = ((), (), s32[]{:S(2)}) async-start(), calls=%async_computation.3 | async-start | bytes 13926400 | tf_op jit(solution)/shard_map/all_gather | solution.py:116
  22.7 9.8 %copy-start.2 = (s32[64]{0:T(128)S(1)}, s32[64]{0:T(128)}, u32[]{:S(2)}) copy-start(s32[64]{0:T(128)} %param.40) | copy-start | bytes 772
  22.7 10.4 %copy-start.3 = (s32[64]{0:T(128)S(1)}, s32[64]{0:T(128)}, u32[]{:S(2)}) copy-start(s32[64]{0:T(128)} %param.42) | copy-start | bytes 772
  22.7 11.1 %copy-start.4 = (s32[16]{0:T(128)S(1)}, s32[16]{0:T(128)}, u32[]{:S(2)}) copy-start(s32[16]{0:T(128)} %param.39) | copy-start | bytes 196
  22.7 11.7 %copy-start.5 = (s32[16]{0:T(128)S(1)}, s32[16]{0:T(128)}, u32[]{:S(2)}) copy-start(s32[16]{0:T(128)} %param.41) | copy-start | bytes 196
  22.7 12.4 %copy-start.25 = (s32[16,16]{1,0:T(8,128)S(1)}, s32[16,16]{1,0:T(8,128)}, u32[]{:S(2)}) copy-start(s32[16,16]{1,0:T(8,128)} %param.36) | copy-start | bytes 3076
  22.7 13.0 %copy-start.6 = (s32[4]{0:T(128)S(1)}, s32[4]{0:T(128)}, u32[]{:S(2)}) copy-start(s32[4]{0:T(128)} %param.38) | copy-start | bytes 52
  22.7 13.7 %copy-start.24 = (s32[4,16]{1,0:T(4,128)S(1)}, s32[4,16]{1,0:T(4,128)}, u32[]{:S(2)}) copy-start(s32[4,16]{1,0:T(4,128)} %param.35) | copy-start | bytes 772
  22.7 14.3 %copy-start.31 = (bf16[2560]{0:T(1024)(128)(2,1)S(1)}, bf16[2560]{0:T(1024)(128)(2,1)}, u32[]{:S(2)}) copy-start(bf16[2560]{0:T(1024)(128)(2,1)} %param.24) | copy-start | bytes 15364
  22.7 105.2 %all-to-all-start = ((bf16[16,8,1,2,80,128]{5,4,3,1,2,0:T(8,128)(2,1)}), bf16[16,8,1,2,80,128]{5,4,3,1,2,0:T(8,128)(2,1)}, u32[]{:S(2)}, u32[]{:S(2)}) async-start(bf16[16,8,1,2,80,128]{5,4,3,1,2,0:T(8,128)(2,1)} %select_select_fusion), calls=%async_computation | async-start | bytes 10485760 | tf_op jit(solution)/shard_map/all_to_all | solution.py:160
  31.1 249.6 %reduce-scatter.3.cloned.1.call-start = ((), (), s32[]{:S(2)}) async-start(), calls=%async_computation.4 | async-start | bytes 5898240 | tf_op jit(solution)/shard_map/reduce_scatter | solution.py:192
  40.4 8.6 %copy-start.19 = (bf16[2560,80]{0,1:T(8,128)(2,1)S(1)}, bf16[2560,80]{0,1:T(8,128)(2,1)}, u32[]{:S(2)}) copy-start(bf16[2560,80]{0,1:T(8,128)(2,1)} %param.27) | copy-start | bytes 1228804
  43.4 11.3 %copy-start.36 = (bf16[2560,80]{0,1:T(8,128)(2,1)S(1)}, bf16[2560,80]{0,1:T(8,128)(2,1)}, u32[]{:S(2)}) copy-start(bf16[2560,80]{0,1:T(8,128)(2,1)} %param.26) | copy-start | bytes 1228804
  65.5 71.2 %copy-start.14 = (pred[128,4,1024]{0,2,1:T(8,128)(4,1)}, pred[128,4,1024]{0,2,1:T(8,128)(4,1)S(1)}, u32[]{:S(2)}) copy-start(pred[128,4,1024]{0,2,1:T(8,128)(4,1)S(1)} %fusion.37) | copy-start | bytes 1572868
  140.0 18.2 %copy-start.30 = (s32[1024]{0:T(1024)S(1)}, s32[1024]{0:T(1024)}, u32[]{:S(2)}) copy-start(s32[1024]{0:T(1024)} %pad_clamp_fusion.4) | copy-start | bytes 12292
  142.7 22.6 %copy-start.29 = (s32[1024]{0:T(1024)S(1)}, s32[1024]{0:T(1024)}, u32[]{:S(2)}) copy-start(s32[1024]{0:T(1024)} %pad_clamp_fusion.5) | copy-start | bytes 12292
  158.2 14.3 %copy-start.34 = (pred[4,16]{1,0:T(4,128)(4,1)S(1)}, pred[4,16]{1,0:T(4,128)(4,1)}, u32[]{:S(2)}) copy-start(pred[4,16]{1,0:T(4,128)(4,1)} %compare_and_fusion.2) | copy-start | bytes 196
  172.5 9.4 %copy-start.33 = (pred[4,16]{1,0:T(4,128)(4,1)S(1)}, pred[4,16]{1,0:T(4,128)(4,1)}, u32[]{:S(2)}) copy-start(pred[4,16]{1,0:T(4,128)(4,1)} %compare_and_fusion.1) | copy-start | bytes 196
  181.8 9.5 %copy-start.12 = (pred[128,4,2048]{0,2,1:T(8,128)(4,1)S(1)}, pred[128,4,2048]{0,2,1:T(8,128)(4,1)}, u32[]{:S(2)}) copy-start(pred[128,4,2048]{0,2,1:T(8,128)(4,1)} %get-tuple-element.26) | copy-start | bytes 3145732
  181.8 9.5 %copy-start.21 = (bf16[128,4,4,40]{0,3,2,1:T(8,128)(2,1)S(1)}, bf16[128,4,4,40]{0,3,2,1:T(8,128)(2,1)}, u32[]{:S(2)}) copy-start(bf16[128,4,4,40]{0,3,2,1:T(8,128)(2,1)} %copy-done.20) | copy-start | bytes 491524
  181.8 9.5 %copy-start.23 = (bf16[128,4,4,40]{0,3,2,1:T(8,128)(2,1)S(1)}, bf16[128,4,4,40]{0,3,2,1:T(8,128)(2,1)}, u32[]{:S(2)}) copy-start(bf16[128,4,4,40]{0,3,2,1:T(8,128)(2,1)} %copy-done.22) | copy-start | bytes 491524
  191.3 8.8 %copy-start.11 = (pred[128,4,2048]{0,2,1:T(8,128)(4,1)S(1)}, pred[128,4,2048]{0,2,1:T(8,128)(4,1)}, u32[]{:S(2)}) copy-start(pred[128,4,2048]{0,2,1:T(8,128)(4,1)} %get-tuple-element.25) | copy-start | bytes 3145732
  191.3 8.8 %copy-start.13 = (bf16[4,1,2,80,2048]{4,3,0,2,1:T(8,128)(2,1)S(1)}, bf16[4,1,2,80,2048]{4,3,0,2,1:T(8,128)(2,1)}, u32[]{:S(2)}) copy-start(bf16[4,1,2,80,2048]{4,3,0,2,1:T(8,128)(2,1)} %reshape.777) | copy-start | bytes 7864324
  200.2 13.6 %slice-start = ((s8[8388608]{0:T(1024)(128)(4,1)}), s8[4194304]{0:T(1024)(128)(4,1)S(1)}, s32[]{:S(2)}) async-start(s8[8388608]{0:T(1024)(128)(4,1)} %bitcast.323), calls=%async_computation.7 | async-start | bytes 8388608
  202.9 10.8 %copy-start.27 = (f32[128,4,4]{0,2,1:T(4,128)S(1)}, f32[128,4,4]{0,2,1:T(4,128)}, u32[]{:S(2)}) copy-start(f32[128,4,4]{0,2,1:T(4,128)} %copy-done.26) | copy-start | bytes 24580
  202.9 10.8 %copy-start.28 = (f32[128,4,4]{0,2,1:T(4,128)S(1)}, f32[128,4,4]{0,2,1:T(4,128)}, u32[]{:S(2)}) copy-start(f32[128,4,4]{0,2,1:T(4,128)} %fusion.15) | copy-start | bytes 24580
  202.9 10.8 %slice-start.1 = ((s8[8388608]{0:T(1024)(128)(4,1)}), s8[4194304]{0:T(1024)(128)(4,1)S(1)}, s32[]{:S(2)}) async-start(s8[8388608]{0:T(1024)(128)(4,1)} %bitcast.323), calls=%async_computation.8 | async-start | bytes 8388608
  202.9 10.8 %copy-start.15 = (pred[128,4,1024]{0,2,1:T(8,128)(4,1)S(1)}, pred[128,4,1024]{0,2,1:T(8,128)(4,1)}, u32[]{:S(2)}) copy-start(pred[128,4,1024]{0,2,1:T(8,128)(4,1)} %copy-done.14) | copy-start | bytes 1572868
  203.0 10.8 %copy-start.16 = (bf16[4,1,2,80,1024]{4,3,0,2,1:T(8,128)(2,1)S(1)}, bf16[4,1,2,80,1024]{4,3,0,2,1:T(8,128)(2,1)}, u32[]{:S(2)}) copy-start(bf16[4,1,2,80,1024]{4,3,0,2,1:T(8,128)(2,1)} %reshape.788) | copy-start | bytes 3932164
  239.6 71.4 %all-gather.5.cloned.1.call-start = ((), (), s32[]{:S(2)}) async-start(), calls=%async_computation.5 | async-start | bytes 2949120 | tf_op jit(solution)/shard_map/all_gather | solution.py:201
  285.2 85.7 %reduce-scatter.5.cloned.1.call-start = ((), (), s32[]{:S(2)}) async-start(), calls=%async_computation.6 | async-start | bytes 5898240 | tf_op jit(solution)/shard_map/reduce_scatter | solution.py:205
  (12 other events, 42.0 us)
Sparse Core Ops, SparseCore 0:
  9.5 148.6 all-gather.2
  239.7 40.9 reduce-scatter.2
  285.4 25.5 all-gather.4
  330.5 40.4 reduce-scatter.4
where the time goes:
time: 387 us; the launch traced here: 381 us
  waiting for transfers between devices  180 us (47%)
  matrix products  65.3 us (17%)
  local copies, waits for them, and re-layouts  59.2 us (15%)
  other arithmetic  54.4 us (14%)
  between operations  13.9 us (4%)
  starting transfers between devices  8.66 us (2%)
    all_to_all x1, waiting for transfers between devices, shards(): lax.all_to_all(outgoing, 'seq', split_axis=0, concat_axis=0, tiled=True)  56.7 us
    reduce_scatter x1, waiting for transfers between devices, shards(): lax.psum_scatter(jnp.dot(activated, w_down, preferred_element_type=jnp.fl...  40.6 us
    reduce_scatter x1, waiting for transfers between devices, shards(): lax.psum_scatter(jnp.dot(attended, w_out, preferred_element_type=jnp.floa...  40.4 us
    all_gather x1, waiting for transfers between devices, shards(): normed_ffn = lax.all_gather(normed_own, 'tp', axis=0, tiled=True)  25.5 us
    dot_general x4, matrix products, attend(): jnp.einsum('nbkgt,bket->nbkge', weights.astype(jnp.bfloat16), key_pack[:,...  21.1 us
    all_gather x1, waiting for transfers between devices, shards(): page_store = lax.all_gather(shared_pages, 'seq', axis=0, tiled=True)  15.5 us
    dot_general x4, matrix products, attend(): jnp.einsum('nbkge,bket->nbkgt', queries, key_pack[:, :, 0], preferred_ele...  14.4 us
    reduce_sum x3, other arithmetic, attend(): totals = jnp.sum(weights, -1)  13.6 us
  transfers between devices with their start and end apart: 5, of which 5 were waited for; matrix products, arithmetic and copies ran while one was open for 17% of the time, Pallas kernels for 0%

commit v1 on v0

--- a/solution.py
+++ b/solution.py
@@ -113,7 +113,9 @@
     new_index = jnp.arange(new_rows, dtype=jnp.int32)
     query_pos = context[None, :] + new_index[:, None]
     all_slots = slot_request.reshape(seq_count, local_reqs)
-    page_store = lax.all_gather(shared_pages, "seq", axis=0, tiled=True)
+    page_store = jnp.concatenate(
+        lax.all_to_all(jnp.stack([shared_pages] * lax.axis_size("seq")), "seq", 0, 0), axis=0
+    )
     root_index = root_table[root_nodes]
     mid_index = mid_table[mid_nodes]
     normed = rms_norm(hidden, gain_attn).reshape(-1, model_width)

time: 387 us -> 542 us (1.40)
  waiting for transfers between devices: 180 us -> 320 us
  local copies, waits for them, and re-layouts: 59.2 us -> 71.7 us
  starting transfers between devices: 8.66 us -> 14.2 us
    all_to_all x0 -> x1, waiting for transfers between devices: none -> 136 us  [shards(): lax.all_to_all(jnp.stack([shared_pages] * lax.axis_size('seq')), 'seq', 0...]
    all_to_all x1, waiting for transfers between devices: 56.7 us -> 77.5 us  [shards(): lax.all_to_all(outgoing, 'seq', split_axis=0, concat_axis=0, tiled=True)]
    all_gather x1 -> x0, waiting for transfers between devices: 15.5 us -> none  [shards(): page_store = lax.all_gather(shared_pages, 'seq', axis=0, tiled=True)]
    another operation x0 -> x1, local copies, waits for them, and re-layouts: none -> 7.28 us  [shards(): jnp.stack([shared_pages] * lax.axis_size('seq'))]
    all_to_all x0 -> x1, starting transfers between devices: none -> 5.48 us  [shards(): lax.all_to_all(jnp.stack([shared_pages] * lax.axis_size('seq')), 'seq', 0...]
  transfers between devices with their start and end apart: 5 -> 5, of which waited for: 5 -> 5; matrix products, arithmetic and copies ran while one was open for 17% -> 9% of each run, Pallas kernels for 0% -> 0%
where the time goes in v1:
time: 542 us; the launch traced here: 535 us
  waiting for transfers between devices  320 us (59%)
  local copies, waits for them, and re-layouts  71.7 us (13%)
  matrix products  65.3 us (12%)
  other arithmetic  49.8 us (9%)
  starting transfers between devices  14.2 us (3%)
  between operations  14.1 us (3%)
    all_to_all x1, waiting for transfers between devices, shards(): lax.all_to_all(jnp.stack([shared_pages] * lax.axis_size('seq')), 'seq', 0...  136 us
    all_to_all x1, waiting for transfers between devices, shards(): lax.all_to_all(outgoing, 'seq', split_axis=0, concat_axis=0, tiled=True)  77.5 us
    reduce_scatter x1, waiting for transfers between devices, shards(): lax.psum_scatter(jnp.dot(activated, w_down, preferred_element_type=jnp.fl...  40.6 us
    reduce_scatter x1, waiting for transfers between devices, shards(): lax.psum_scatter(jnp.dot(attended, w_out, preferred_element_type=jnp.floa...  40 us
    all_gather x1, waiting for transfers between devices, shards(): normed_ffn = lax.all_gather(normed_own, 'tp', axis=0, tiled=True)  25.4 us
    dot_general x4, matrix products, attend(): jnp.einsum('nbkgt,bket->nbkge', weights.astype(jnp.bfloat16), key_pack[:,...  21.1 us
    dot_general x4, matrix products, attend(): jnp.einsum('nbkge,bket->nbkgt', queries, key_pack[:, :, 0], preferred_ele...  14.4 us
    reduce_sum x3, other arithmetic, attend(): totals = jnp.sum(weights, -1)  13.6 us
  transfers between devices with their start and end apart: 5, of which 5 were waited for; matrix products, arithmetic and copies ran while one was open for 9% of the time, Pallas kernels for 0%

profile of v1, /device:TPU:0, one launch (start us, length us, event | category | flops | bytes accessed | tf_op | source)
XLA Modules:
  0.0 534.7 jit_solution(1668870124835671392)
XLA Ops:
  13.0 3.6 gather_fusion.11
  16.6 5.5 %select_select_fusion = bf16[16,8,1,2,80,128]{5,4,3,1,2,0:T(8,128)(2,1)} fusion(bf16[16,8,1,2,80,128]{5,4,3,1,2,0:T(8,128)(2,1)} %bitcast.322, pred[16]{0:T(512)(128)(4,1)S(1)} %reduce_or.9, pred[16,8]{1,0:T(8,128)(4,1)S(1)} %get-tuple-element.15), kind=kLoop, calls=%fused_computation.44 | loop fusion | flops 5242880 | bytes 10485904 | tf_op jit(solution)/shard_map/jit(_where)/select_n | solution.py:159
  22.1 8.3 %all-to-all-start.1 = ((bf16[16,8,1,2,80,128]{5,4,3,1,2,0:T(8,128)(2,1)}), bf16[16,8,1,2,80,128]{5,4,3,1,2,0:T(8,128)(2,1)}, u32[]{:S(2)}, u32[]{:S(2)}) async-start(bf16[16,8,1,2,80,128]{5,4,3,1,2,0:T(8,128)(2,1)} %select_select_fusion), calls=%async_computation.1 | async-start | bytes 10485760 | tf_op jit(solution)/shard_map/all_to_all | solution.py:162
  31.1 77.5 %all-to-all-done.1 = bf16[16,8,1,2,80,128]{5,4,3,1,2,0:T(8,128)(2,1)} async-done(((bf16[16,8,1,2,80,128]{5,4,3,1,2,0:T(8,128)(2,1)}), bf16[16,8,1,2,80,128]{5,4,3,1,2,0:T(8,128)(2,1)}, u32[]{:S(2)}, u32[]{:S(2)}) %all-to-all-start.1) | async-done | bytes 5242912 | tf_op jit(solution)/shard_map/all_to_all | solution.py:162
  108.6 7.3 %stack.2 = bf16[16,20,1,2,80,128]{5,4,3,2,1,0:T(8,128)(2,1)} broadcast(bf16[20,2,80,128]{3,2,1,0:T(8,128)(2,1)S(1)} %bitcast.328), dimensions={1,3,4,5} | broadcast | bytes 13926400 | tf_op jit(solution)/shard_map/stack | solution.py:117
  116.0 5.5 %all-to-all-start = ((bf16[16,20,1,2,80,128]{5,4,3,2,1,0:T(8,128)(2,1)}), bf16[16,20,1,2,80,128]{5,4,3,2,1,0:T(8,128)(2,1)}, u32[]{:S(2)}, u32[]{:S(2)}) async-start(bf16[16,20,1,2,80,128]{5,4,3,2,1,0:T(8,128)(2,1)} %stack.2), calls=%async_computation | async-start | bytes 26214400 | tf_op jit(solution)/shard_map/all_to_all | solution.py:117
  126.8 3.3 fusion.17
  130.1 3.0 fusion.19
  133.1 5.8 %reshape.800 = bf16[512,2560]{1,0:T(8,128)(2,1)} reshape(bf16[128,4,2560]{2,1,0:T(4,128)(2,1)} %fusion.19) | data formatting | bytes 5242880 | tf_op jit(solution)/shard_map/reshape | solution.py:121
  138.9 2.6 convolution_convert_fusion
  144.8 2.8 fusion.71
  155.4 5.5 %fusion.26 = (pred[128,4,2048]{0,2,1:T(8,128)(4,1)}, pred[128,4,2048]{0,2,1:T(8,128)(4,1)}) fusion(s32[128,4]{0,1:T(4,128)S(1)} %get-tuple-element.27, pred[4,2048]{1,0:T(4,128)(4,1)S(1)} %iota_compare_fusion.1, s32[4,2048]{1,0:T(4,128)S(1)} %iota_add_fusion, pred[4,2048]{1,0:T(4,128)(4,1)S(1)} %iota_compare_fusion), kind=kLoop, calls=%fused_computation.51 | loop fusion | flops 10485760 | bytes 2148352 | tf_op jit(solution)/shard_map/and | solution.py:47
  160.9 3.4 gather_fusion.12
  169.6 3.2 copy-done.10
  172.9 2.7 fusion.15
  175.6 136.0 %all-to-all-done = bf16[16,20,1,2,80,128]{5,4,3,2,1,0:T(8,128)(2,1)} async-done(((bf16[16,20,1,2,80,128]{5,4,3,2,1,0:T(8,128)(2,1)}), bf16[16,20,1,2,80,128]{5,4,3,2,1,0:T(8,128)(2,1)}, u32[]{:S(2)}, u32[]{:S(2)}) %all-to-all-start) | async-done | bytes 13107232 | tf_op jit(solution)/shard_map/all_to_all | solution.py:117
  311.6 7.1 %gather_fusion.15 = bf16[64,2,80,128]{3,2,1,0:T(8,128)(2,1)} fusion(bf16[320,2,80,128]{3,2,1,0:T(8,128)(2,1)} %bitcast.9, s32[1024]{0:T(1024)S(1)} %copy-done.31), kind=kCustom, calls=%fused_computation.1.clone | custom fusion | bytes 5243136 | tf_op jit(solution)/shard_map/jit(_take)/gather | solution.py:177
  318.7 7.1 %gather_fusion.14 = bf16[64,2,80,128]{3,2,1,0:T(8,128)(2,1)} fusion(bf16[320,2,80,128]{3,2,1,0:T(8,128)(2,1)} %bitcast.9, s32[1024]{0:T(1024)S(1)} %copy-done.30), kind=kCustom, calls=%fused_computation.clone | custom fusion | bytes 5243136 | tf_op jit(solution)/shard_map/jit(_take)/gather | solution.py:168
  330.4 5.2 reshape.784
  340.1 5.2 reshape.788
  345.3 8.8 %fusion.1 = (f32[128,4,4]{0,2,1:T(4,128)S(1)}, f32[4,2048,128,4]{2,1,3,0:T(8,128)}) fusion(pred[128,4,2048]{0,2,1:T(8,128)(4,1)S(1)} %copy-done.12, bf16[128,4,4,40]{0,3,2,1:T(8,128)(2,1)S(1)} %copy-done.24, bf16[128,4,4,40]{0,3,2,1:T(8,128)(2,1)S(1)} %copy-done.22, bf16[4,1,2,80,2048]{4,3,0,2,1:T(8,128)(2,1)} %reshape.788), kind=kOutput, calls=%fused_computation.21 | convolution fusion | flops 684324864 | bytes 19472384 | tf_op jit(solution)/shard_map/nbkge,bket->nbkgt/dot_general | solution.py:43
  354.2 2.7 fusion
  357.0 10.7 %fusion.2 = (f32[128,4,4]{0,2,1:T(4,128)S(1)}, f32[128,4,4]{0,2,1:T(4,128)S(1)}) fusion(f32[4,2048,128,4]{2,1,3,0:T(8,128)S(1)} %get-tuple-element.36, f32[128,4,4]{0,2,1:T(4,128)S(1)} %get-tuple-element.35, pred[128,4,2048]{0,2,1:T(8,128)(4,1)S(1)} %copy-done.11, f32[128,4,4]{0,2,1:T(4,128)S(1)} %get-tuple-element.29, ...), kind=kLoop, calls=%fused_computation.22 | loop fusion | flops 41938944 | bytes 35684352 | tf_op jit(solution)/shard_map/reduce_sum | solution.py:51
  367.8 3.0 fusion.54
  370.8 10.7 %fusion.66 = f32[128,4,1,4,80]{0,4,3,1,2:T(8,128)} fusion(f32[4,2048,128,4]{2,1,3,0:T(8,128)} %get-tuple-element.30, f32[128,4,4]{0,2,1:T(4,128)S(1)} %get-tuple-element.29, pred[128,4,2048]{0,2,1:T(8,128)(4,1)S(1)} %copy-done.12, bf16[4,1,2,80,2048]{4,3,0,2,1:T(8,128)(2,1)} %reshape.788, f32[128,4,4]{0,2,1:T(4,128)S(1)} %bitcast.343), kind=kOutput, calls=%fused_computation.89 | convolution fusion | flops 692224000 | bytes 19808256 | tf_op jit(solution)/shard_map/nbkgt,bket->nbkge/dot_general | solution.py:52
  381.4 5.8 %fusion.63 = f32[128,4,1,4,80]{0,4,3,1,2:T(8,128)} fusion(f32[128,4,1,4,80]{0,4,3,1,2:T(8,128)} %fusion.66, f32[4,2048,128,4]{2,1,3,0:T(8,128)S(1)} %get-tuple-element.36, f32[128,4,4]{0,2,1:T(4,128)S(1)} %get-tuple-element.35, pred[128,4,2048]{0,2,1:T(8,128)(4,1)S(1)} %copy-done.11, bf16[4,1,2,80,2048]{4,3,0,2,1:T(8,128)(2,1)} %reshape.784, ...), kind=kOutput, calls=%fused_computation.88 | convolution fusion | flops 692551680 | bytes 20471808 | tf_op jit(solution)/shard_map/nbkgt,bket->nbkge/dot_general | solution.py:52
  389.7 3.8 fusion.122
  394.3 40.0 %reduce-scatter.3.cloned.1.call-done = f32[64,2560]{1,0:T(8,128)} async-done(((f32[512,2560]{1,0:T(8,128)}), f32[64,2560]{1,0:T(8,128)}) %reduce-scatter.3.cloned.1.call-update) | async-done | bytes 655376 | tf_op jit(solution)/shard_map/reduce_scatter | solution.py:194
  439.2 25.4 %all-gather.2.cloned.1.call-done = bf16[512,2560]{1,0:T(8,128)(2,1)} async-done(((bf16[64,2560]{1,0:T(8,128)(2,1)}), bf16[512,2560]{1,0:T(8,128)(2,1)}) %all-gather.2.cloned.1.call-update) | async-done | bytes 2621456 | tf_op jit(solution)/shard_map/all_gather | solution.py:203
  464.6 6.8 %fusion.123 = f32[512,864]{0,1:T(8,128)} fusion(bf16[512,2560]{1,0:T(8,128)(2,1)} %all-gather.2.cloned.1.call-done, bf16[2560,864]{0,1:T(8,128)(2,1)} %param.30), kind=kOutput, calls=%fused_computation.212 | convolution fusion | flops 2264924160 | bytes 8814592 | tf_op jit(solution)/shard_map/dot_general | solution.py:204
  471.5 12.5 %fusion.76 = f32[512,2560]{1,0:T(8,128)} fusion(bf16[864,2560]{1,0:T(8,128)(2,1)} %param.32, f32[512,864]{0,1:T(8,128)} %fusion.123, bf16[512,2560]{1,0:T(8,128)(2,1)} %all-gather.2.cloned.1.call-done, bf16[2560,864]{0,1:T(8,128)(2,1)} %param.31), kind=kOutput, calls=%fused_computation.97 | convolution fusion | flops 4532502528 | bytes 18481152 | tf_op jit(solution)/shard_map/dot_general | solution.py:208
  484.0 40.6 %reduce-scatter.5.cloned.1.call-done = f32[64,2560]{1,0:T(8,128)} async-done(((f32[512,2560]{1,0:T(8,128)}), f32[64,2560]{1,0:T(8,128)}) %reduce-scatter.5.cloned.1.call-update) | async-done | bytes 655376 | tf_op jit(solution)/shard_map/reduce_scatter | solution.py:207
  (181 shorter events, 49.0 us)
Async XLA Ops:
  6.5 383.2 %copy-start = (bf16[320,2560]{1,0:T(8,128)(2,1)S(1)}, bf16[320,2560]{1,0:T(8,128)(2,1)}, u32[]{:S(2)}) copy-start(bf16[320,2560]{1,0:T(8,128)(2,1)} %param.28) | copy-start | bytes 4915204
  22.1 8.4 %copy-start.1 = (s32[64]{0:T(128)S(1)}, s32[64]{0:T(128)}, u32[]{:S(2)}) copy-start(s32[64]{0:T(128)} %param.43) | copy-start | bytes 772
  22.1 86.5 %copy-start.19 = (bf16[20,1,2,80,128]{4,3,2,1,0:T(8,128)(2,1)S(1)}, bf16[20,1,2,80,128]{4,3,2,1,0:T(8,128)(2,1)}, u32[]{:S(2)}) copy-start(bf16[20,1,2,80,128]{4,3,2,1,0:T(8,128)(2,1)} %param.33) | copy-start | bytes 2457604
  22.1 86.5 %all-to-all-start.1 = ((bf16[16,8,1,2,80,128]{5,4,3,1,2,0:T(8,128)(2,1)}), bf16[16,8,1,2,80,128]{5,4,3,1,2,0:T(8,128)(2,1)}, u32[]{:S(2)}, u32[]{:S(2)}) async-start(bf16[16,8,1,2,80,128]{5,4,3,1,2,0:T(8,128)(2,1)} %select_select_fusion), calls=%async_computation.1 | async-start | bytes 10485760 | tf_op jit(solution)/shard_map/all_to_all | solution.py:162
  115.9 7.6 %copy-start.4 = (s32[16]{0:T(128)S(1)}, s32[16]{0:T(128)}, u32[]{:S(2)}) copy-start(s32[16]{0:T(128)} %param.39) | copy-start | bytes 196
  115.9 8.2 %copy-start.5 = (s32[16]{0:T(128)S(1)}, s32[16]{0:T(128)}, u32[]{:S(2)}) copy-start(s32[16]{0:T(128)} %param.41) | copy-start | bytes 196
  115.9 8.8 %copy-start.26 = (s32[16,16]{1,0:T(8,128)S(1)}, s32[16,16]{1,0:T(8,128)}, u32[]{:S(2)}) copy-start(s32[16,16]{1,0:T(8,128)} %param.36) | copy-start | bytes 3076
  115.9 9.5 %copy-start.6 = (s32[4]{0:T(128)S(1)}, s32[4]{0:T(128)}, u32[]{:S(2)}) copy-start(s32[4]{0:T(128)} %param.38) | copy-start | bytes 52
  115.9 10.1 %copy-start.25 = (s32[4,16]{1,0:T(4,128)S(1)}, s32[4,16]{1,0:T(4,128)}, u32[]{:S(2)}) copy-start(s32[4,16]{1,0:T(4,128)} %param.35) | copy-start | bytes 772
  116.0 10.8 %copy-start.32 = (bf16[2560]{0:T(1024)(128)(2,1)S(1)}, bf16[2560]{0:T(1024)(128)(2,1)}, u32[]{:S(2)}) copy-start(bf16[2560]{0:T(1024)(128)(2,1)} %param.24) | copy-start | bytes 15364
  116.0 195.6 %all-to-all-start = ((bf16[16,20,1,2,80,128]{5,4,3,2,1,0:T(8,128)(2,1)}), bf16[16,20,1,2,80,128]{5,4,3,2,1,0:T(8,128)(2,1)}, u32[]{:S(2)}, u32[]{:S(2)}) async-start(bf16[16,20,1,2,80,128]{5,4,3,2,1,0:T(8,128)(2,1)} %stack.2), calls=%async_computation | async-start | bytes 26214400 | tf_op jit(solution)/shard_map/all_to_all | solution.py:117
  121.5 312.8 %reduce-scatter.3.cloned.1.call-start = ((), (), s32[]{:S(2)}) async-start(), calls=%async_computation.4 | async-start | bytes 5898240 | tf_op jit(solution)/shard_map/reduce_scatter | solution.py:194
  130.1 8.8 %copy-start.20 = (bf16[2560,80]{0,1:T(8,128)(2,1)S(1)}, bf16[2560,80]{0,1:T(8,128)(2,1)}, u32[]{:S(2)}) copy-start(bf16[2560,80]{0,1:T(8,128)(2,1)} %param.27) | copy-start | bytes 1228804
  133.1 11.7 %copy-start.37 = (bf16[2560,80]{0,1:T(8,128)(2,1)S(1)}, bf16[2560,80]{0,1:T(8,128)(2,1)}, u32[]{:S(2)}) copy-start(bf16[2560,80]{0,1:T(8,128)(2,1)} %param.26) | copy-start | bytes 1228804
  155.2 14.5 %copy-start.14 = (pred[128,4,1024]{0,2,1:T(8,128)(4,1)}, pred[128,4,1024]{0,2,1:T(8,128)(4,1)S(1)}, u32[]{:S(2)}) copy-start(pred[128,4,1024]{0,2,1:T(8,128)(4,1)S(1)} %fusion.35) | copy-start | bytes 1572868
  172.9 138.7 %copy-start.31 = (s32[1024]{0:T(1024)S(1)}, s32[1024]{0:T(1024)}, u32[]{:S(2)}) copy-start(s32[1024]{0:T(1024)} %pad_clamp_fusion.4) | copy-start | bytes 12292
  175.5 143.1 %copy-start.30 = (s32[1024]{0:T(1024)S(1)}, s32[1024]{0:T(1024)}, u32[]{:S(2)}) copy-start(s32[1024]{0:T(1024)} %pad_clamp_fusion.5) | copy-start | bytes 12292
  311.6 14.2 %copy-start.35 = (pred[4,16]{1,0:T(4,128)(4,1)S(1)}, pred[4,16]{1,0:T(4,128)(4,1)}, u32[]{:S(2)}) copy-start(pred[4,16]{1,0:T(4,128)(4,1)} %compare_and_fusion.2) | copy-start | bytes 196
  327.8 7.7 %copy-start.34 = (pred[4,16]{1,0:T(4,128)(4,1)S(1)}, pred[4,16]{1,0:T(4,128)(4,1)}, u32[]{:S(2)}) copy-start(pred[4,16]{1,0:T(4,128)(4,1)} %compare_and_fusion.1) | copy-start | bytes 196
  337.6 7.7 %copy-start.12 = (pred[128,4,2048]{0,2,1:T(8,128)(4,1)S(1)}, pred[128,4,2048]{0,2,1:T(8,128)(4,1)}, u32[]{:S(2)}) copy-start(pred[128,4,2048]{0,2,1:T(8,128)(4,1)} %get-tuple-element.26) | copy-start | bytes 3145732
  337.6 7.7 %copy-start.22 = (bf16[128,4,4,40]{0,3,2,1:T(8,128)(2,1)S(1)}, bf16[128,4,4,40]{0,3,2,1:T(8,128)(2,1)}, u32[]{:S(2)}) copy-start(bf16[128,4,4,40]{0,3,2,1:T(8,128)(2,1)} %copy-done.21) | copy-start | bytes 491524
  337.6 7.7 %copy-start.24 = (bf16[128,4,4,40]{0,3,2,1:T(8,128)(2,1)S(1)}, bf16[128,4,4,40]{0,3,2,1:T(8,128)(2,1)}, u32[]{:S(2)}) copy-start(bf16[128,4,4,40]{0,3,2,1:T(8,128)(2,1)} %copy-done.23) | copy-start | bytes 491524
  345.3 8.8 %copy-start.11 = (pred[128,4,2048]{0,2,1:T(8,128)(4,1)S(1)}, pred[128,4,2048]{0,2,1:T(8,128)(4,1)}, u32[]{:S(2)}) copy-start(pred[128,4,2048]{0,2,1:T(8,128)(4,1)} %get-tuple-element.25) | copy-start | bytes 3145732
  345.3 8.8 %copy-start.13 = (bf16[4,1,2,80,2048]{4,3,0,2,1:T(8,128)(2,1)S(1)}, bf16[4,1,2,80,2048]{4,3,0,2,1:T(8,128)(2,1)}, u32[]{:S(2)}) copy-start(bf16[4,1,2,80,2048]{4,3,0,2,1:T(8,128)(2,1)} %reshape.784) | copy-start | bytes 7864324
  354.1 13.6 %slice-start = ((s8[8388608]{0:T(1024)(128)(4,1)}), s8[4194304]{0:T(1024)(128)(4,1)S(1)}, s32[]{:S(2)}) async-start(s8[8388608]{0:T(1024)(128)(4,1)} %bitcast.326), calls=%async_computation.7 | async-start | bytes 8388608
  356.9 10.8 %copy-start.28 = (f32[128,4,4]{0,2,1:T(4,128)S(1)}, f32[128,4,4]{0,2,1:T(4,128)}, u32[]{:S(2)}) copy-start(f32[128,4,4]{0,2,1:T(4,128)} %copy-done.27) | copy-start | bytes 24580
  356.9 10.8 %copy-start.29 = (f32[128,4,4]{0,2,1:T(4,128)S(1)}, f32[128,4,4]{0,2,1:T(4,128)}, u32[]{:S(2)}) copy-start(f32[128,4,4]{0,2,1:T(4,128)} %fusion.15) | copy-start | bytes 24580
  356.9 10.8 %slice-start.1 = ((s8[8388608]{0:T(1024)(128)(4,1)}), s8[4194304]{0:T(1024)(128)(4,1)S(1)}, s32[]{:S(2)}) async-start(s8[8388608]{0:T(1024)(128)(4,1)} %bitcast.326), calls=%async_computation.8 | async-start | bytes 8388608
  356.9 10.8 %copy-start.15 = (pred[128,4,1024]{0,2,1:T(8,128)(4,1)S(1)}, pred[128,4,1024]{0,2,1:T(8,128)(4,1)}, u32[]{:S(2)}) copy-start(pred[128,4,1024]{0,2,1:T(8,128)(4,1)} %copy-done.14) | copy-start | bytes 1572868
  356.9 10.8 %copy-start.16 = (bf16[4,1,2,80,1024]{4,3,0,2,1:T(8,128)(2,1)S(1)}, bf16[4,1,2,80,1024]{4,3,0,2,1:T(8,128)(2,1)}, u32[]{:S(2)}) copy-start(bf16[4,1,2,80,1024]{4,3,0,2,1:T(8,128)(2,1)} %reshape.795) | copy-start | bytes 3932164
  393.6 71.0 %all-gather.2.cloned.1.call-start = ((), (), s32[]{:S(2)}) async-start(), calls=%async_computation.5 | async-start | bytes 2949120 | tf_op jit(solution)/shard_map/all_gather | solution.py:203
  438.9 85.7 %reduce-scatter.5.cloned.1.call-start = ((), (), s32[]{:S(2)}) async-start(), calls=%async_computation.6 | async-start | bytes 5898240 | tf_op jit(solution)/shard_map/reduce_scatter | solution.py:207
  (13 other events, 46.9 us)
Sparse Core Ops, SparseCore 0:
  393.7 40.5 reduce-scatter.2
  439.0 25.5 all-gather.1
  484.1 40.4 reduce-scatter.4
